TPU v7x, 256 devices: a whole 4x4x8 slice. The times are simulated.
256 devices in a mesh: dp: 16 (over y, x), expert: 16 (over z, core).
Axes of the slice: x: 4, y: 4, z: 8, core: 2. Of those that a mesh axis runs over, the one named last changes fastest.
Arguments:
- tokens: bfloat16 [32768, 768], P(('dp', 'expert')), may hold values from -6 to 6
- cotangent: bfloat16 [32768, 768], P(('dp', 'expert')), may hold values from -6 to 6
- routes: int32 [32768, 2], P(('dp', 'expert')), may hold values from 0 to 15, all different within a row; in each aligned block of 128 rows (0 to 127, 128 to 255, ...) at most 48 rows name the same one
- gates: float32 [32768, 2], P(('dp', 'expert')), may hold values from 0.1 to 1
- w_in: bfloat16 [16, 2304, 768], P('expert', 'dp'), may hold values from -0.21875 to 0.21875
- w_out: bfloat16 [16, 2304, 768], P('expert', 'dp'), may hold values from -0.125 to 0.125
Outputs:
- d_tokens: bfloat16 [32768, 768], P(('dp', 'expert'))
- grad_in: float32 [16, 2304, 768], P('expert', 'dp')
- grad_out: float32 [16, 2304, 768], P('expert', 'dp')
Inputs may be any that keep to these rules, and one draw needn't show every extreme that they name: `routes`: within the rows of one device (128 rows) no expert is named more than 48 times, and in every draw some expert is named exactly 48 times by the rows of some device; the 2 entries of a row differ.
All inputs are finite; a program needn't handle non-finite values.
Results may differ from a plain program's by a relative error of at most 0.015.
Values may be sent and summed in bfloat16 or wider, within the bound.
No kernel may reach another device: no remote copies, remote signals or barrier semaphores. Data moves between devices by JAX's collectives and lax.ppermute only.
A program may use at most 64 MiB of HBM per device.

v0:
```python
import jax
import jax.numpy as jnp
from jax import lax
from jax.sharding import PartitionSpec as P

tanh_coef = 0.7978845608028654
cubic_coef = 0.044715


def gelu_tanh(value):
    inner = tanh_coef * (value + cubic_coef * value * value * value)
    return 0.5 * value * (1.0 + jnp.tanh(inner))


def gelu_slope(value):
    inner = tanh_coef * (value + cubic_coef * value * value * value)
    slope_t = jnp.tanh(inner)
    return 0.5 * (1.0 + slope_t) + 0.5 * value * (1.0 - slope_t * slope_t) * tanh_coef * (
        1.0 + 3.0 * cubic_coef * value * value
    )


def dispatch_tables(route_blk, gate_blk, experts, capacity):
    tok_rows = route_blk.shape[0]
    flat = route_blk.reshape(-1)
    onehot = (flat[:, None] == jnp.arange(experts, dtype=jnp.int32)[None, :]).astype(jnp.int32)
    before = jnp.cumsum(onehot, axis=0) - onehot
    position = jnp.sum(before * onehot, axis=1)
    slots = (flat * capacity + position).reshape(tok_rows, -1)
    slot_ids = jnp.arange(experts * capacity, dtype=jnp.int32)
    placed = slot_ids[:, None, None] == slots[None, :, :]
    route_mat = jnp.sum(placed.astype(jnp.int32), axis=2).astype(jnp.bfloat16)
    gate_slot = jnp.sum(jnp.where(placed, gate_blk[None, :, :], jnp.float32(0.0)), axis=(1, 2))
    return (route_mat, gate_slot)


def shards(tokens, cotangent, routes, gates, w_in, w_out):
    experts = lax.axis_size("expert")
    tok_rows, model_width = tokens.shape
    top_count = routes.shape[1]
    capacity = 3 * tok_rows * top_count // experts
    shard_rows = w_in.shape[1]
    slot_rows = experts * capacity
    route_mat, gate_slot = dispatch_tables(routes, gates, experts, capacity)
    rows_sent = jnp.dot(route_mat, tokens, preferred_element_type=jnp.float32).astype(jnp.bfloat16)
    grad_rows = jnp.dot(route_mat, cotangent, preferred_element_type=jnp.float32)
    grads_sent = (gate_slot[:, None] * grad_rows).astype(jnp.bfloat16)
    rows_recv, grads_recv = (
        lax.all_to_all(
            rows_sent.reshape(experts, capacity, model_width),
            "expert",
            split_axis=0,
            concat_axis=0,
            tiled=True,
        ),
        lax.all_to_all(
            grads_sent.reshape(experts, capacity, model_width),
            "expert",
            split_axis=0,
            concat_axis=0,
            tiled=True,
        ),
    )
    rows_in = rows_recv.reshape(slot_rows, model_width)
    grads_in = grads_recv.reshape(slot_rows, model_width)
    piece_in = lax.all_gather(w_in[0], "dp", axis=0, tiled=True)
    piece_out = lax.all_gather(w_out[0], "dp", axis=0, tiled=True)
    pre = lax.dot_general(
        rows_in, piece_in, (((1,), (1,)), ((), ())), preferred_element_type=jnp.float32
    )
    acts = gelu_tanh(pre).astype(jnp.bfloat16)
    grad_act = lax.dot_general(
        grads_in, piece_out, (((1,), (1,)), ((), ())), preferred_element_type=jnp.float32
    )
    dpre = (grad_act * gelu_slope(pre)).astype(jnp.bfloat16)
    slot_sum = jnp.dot(dpre, piece_in, preferred_element_type=jnp.float32)
    slot_sum, acts_all, dpre_all = (slot_sum, acts, dpre)
    returned = lax.all_to_all(
        slot_sum.astype(jnp.bfloat16).reshape(experts, capacity, model_width),
        "expert",
        split_axis=0,
        concat_axis=0,
        tiled=True,
    )
    token_grads = lax.dot_general(
        route_mat,
        returned.reshape(slot_rows, model_width),
        (((0,), (0,)), ((), ())),
        preferred_element_type=jnp.float32,
    )
    d_tokens = token_grads.astype(jnp.bfloat16)
    term_in = lax.dot_general(
        dpre_all, rows_in, (((0,), (0,)), ((), ())), preferred_element_type=jnp.float32
    )
    term_out = lax.dot_general(
        acts_all, grads_in, (((0,), (0,)), ((), ())), preferred_element_type=jnp.float32
    )
    summed = lax.psum(
        jnp.concatenate([term_in, term_out], axis=1).astype(jnp.bfloat16), "dp"
    ).astype(jnp.float32)
    own_rows = lax.dynamic_slice_in_dim(summed, lax.axis_index("dp") * shard_rows, shard_rows, 0)
    grad_in = own_rows[:, :model_width][None]
    grad_out = own_rows[:, model_width:][None]
    return (d_tokens, grad_in, grad_out)


def solution(mesh):
    in_specs = (
        P(("dp", "expert"), None),
        P(("dp", "expert"), None),
        P(("dp", "expert"), None),
        P(("dp", "expert"), None),
        P("expert", "dp", None),
        P("expert", "dp", None),
    )
    out_specs = (P(("dp", "expert"), None), P("expert", "dp", None), P("expert", "dp", None))
    return jax.shard_map(shards, mesh=mesh, in_specs=in_specs, out_specs=out_specs, check_vma=False)
```

profile of v0, /device:TPU:32, one launch (start us, length us, event | category | flops | bytes accessed | tf_op | source)
XLA Modules:
  0.0 293.4 jit_solution(5425610005325512928)
XLA Ops:
  8.7 0.8 copy.29
  10.9 0.7 multiply_add_fusion.1
  11.7 1.5 convolution_convert_fusion.2
  13.2 8.6 %all-to-all-start.1 = ((bf16[16,48,768]{2,1,0:T(8,128)(2,1)}), bf16[16,48,768]{2,1,0:T(8,128)(2,1)S(1)}, u32[]{:S(2)}, u32[]{:S(2)}) async-start(bf16[16,48,768]{2,1,0:T(8,128)(2,1)} %bitcast.4), calls=%async_computation.1 | async-start | bytes 2359296 | tf_op jit(solution)/shard_map/all_to_all | solution.py:49
  22.0 1.5 multiply_convert_fusion.2
  23.5 25.9 %all-to-all-done.1 = bf16[16,48,768]{2,1,0:T(8,128)(2,1)S(1)} async-done(((bf16[16,48,768]{2,1,0:T(8,128)(2,1)}), bf16[16,48,768]{2,1,0:T(8,128)(2,1)S(1)}, u32[]{:S(2)}, u32[]{:S(2)}) %all-to-all-start.1) | async-done | bytes 1179680 | tf_op jit(solution)/shard_map/all_to_all | solution.py:49
  49.4 6.7 %all-to-all-start = ((bf16[16,48,768]{2,1,0:T(8,128)(2,1)}), bf16[16,48,768]{2,1,0:T(8,128)(2,1)S(1)}, u32[]{:S(2)}, u32[]{:S(2)}) async-start(bf16[16,48,768]{2,1,0:T(8,128)(2,1)} %bitcast.1), calls=%async_computation | async-start | bytes 2359296 | tf_op jit(solution)/shard_map/all_to_all | solution.py:56
  56.3 11.1 %all-gather.7.cloned.1.call-done = bf16[1,2304,768]{2,1,0:T(8,128)(2,1)} async-done(((bf16[1,144,768]{2,1,0:T(8,128)(2,1)}), bf16[1,2304,768]{2,1,0:T(8,128)(2,1)}) %all-gather.7.cloned.1.call-update) | async-done | bytes 3538960 | tf_op jit(solution)/shard_map/all_gather | solution.py:66
  67.4 7.0 %fusion.9 = f32[768,2304]{1,0:T(8,128)} fusion(bf16[768,768]{1,0:T(8,128)(2,1)S(1)} %bitcast.49, bf16[1,2304,768]{2,1,0:T(8,128)(2,1)} %all-gather.7.cloned.1.call-done), kind=kOutput, calls=%fused_computation.15 | convolution fusion | flops 2717908992 | bytes 11796480 | tf_op jit(solution)/shard_map/dot_general | solution.py:68
  74.3 9.3 %all-to-all-done = bf16[16,48,768]{2,1,0:T(8,128)(2,1)S(1)} async-done(((bf16[16,48,768]{2,1,0:T(8,128)(2,1)}), bf16[16,48,768]{2,1,0:T(8,128)(2,1)S(1)}, u32[]{:S(2)}, u32[]{:S(2)}) %all-to-all-start) | async-done | bytes 1179680 | tf_op jit(solution)/shard_map/all_to_all | solution.py:56
  83.6 8.3 %convolution_convert_fusion = bf16[2304,768]{0,1:T(8,128)(2,1)} fusion(bf16[768,768]{1,0:T(8,128)(2,1)S(1)} %bitcast.51, f32[768,2304]{1,0:T(8,128)} %fusion.9), kind=kOutput, calls=%fused_computation.11 | convolution fusion | flops 2735603712 | bytes 11796480 | tf_op jit(solution)/shard_map/dot_general | solution.py:95
  91.9 31.2 %all-gather.5.cloned.1.call-done = bf16[1,2304,768]{2,1,0:T(8,128)(2,1)} async-done(((bf16[1,144,768]{2,1,0:T(8,128)(2,1)}), bf16[1,2304,768]{2,1,0:T(8,128)(2,1)}) %all-gather.5.cloned.1.call-update) | async-done | bytes 3538960 | tf_op jit(solution)/shard_map/all_gather | solution.py:67
  123.2 8.4 %fusion.6 = bf16[768,2304]{1,0:T(8,128)(2,1)S(1)} fusion(f32[768,2304]{1,0:T(8,128)} %fusion.9, bf16[768,768]{1,0:T(8,128)(2,1)S(1)} %bitcast.52, bf16[1,2304,768]{2,1,0:T(8,128)(2,1)} %all-gather.5.cloned.1.call-done), kind=kOutput, calls=%fused_computation.8 | convolution fusion | flops 2751528960 | bytes 15335424 | tf_op jit(solution)/shard_map/dot_general | solution.py:72
  131.6 1.7 copy-done.3
  133.4 4.7 %convolution_convert_fusion.1 = bf16[2304,768]{0,1:T(8,128)(2,1)} fusion(bf16[768,2304]{1,0:T(8,128)(2,1)S(1)} %fusion.6, bf16[768,768]{1,0:T(8,128)(2,1)S(1)} %bitcast.50), kind=kOutput, calls=%fused_computation.12 | convolution fusion | flops 2719678464 | bytes 8257536 | tf_op jit(solution)/shard_map/dot_general | solution.py:92
  138.0 6.4 %pad_maximum_fusion = bf16[2304,1536]{0,1:T(8,128)(2,1)} fusion(bf16[2304,768]{0,1:T(8,128)(2,1)} %convolution_convert_fusion, bf16[2304,768]{0,1:T(8,128)(2,1)} %convolution_convert_fusion.1), kind=kLoop, calls=%fused_computation.9 | loop fusion | flops 14155776 | bytes 14155776 | tf_op jit(solution)/shard_map/concatenate | solution.py:99
  144.5 7.0 %fusion.16 = bf16[768,768]{1,0:T(8,128)(2,1)} fusion(bf16[768,2304]{1,0:T(8,128)(2,1)} %copy-done.3, bf16[1,2304,768]{2,1,0:T(8,128)(2,1)} %all-gather.7.cloned.1.call-done), kind=kOutput, calls=%fused_computation.23 | convolution fusion | flops 2718498816 | bytes 8257536 | tf_op jit(solution)/shard_map/dot_general | solution.py:76
  151.5 7.5 %all-to-all-start.2 = ((bf16[16,48,768]{2,1,0:T(8,128)(2,1)}), bf16[16,48,768]{2,1,0:T(8,128)(2,1)S(1)}, u32[]{:S(2)}, u32[]{:S(2)}) async-start(bf16[16,48,768]{2,1,0:T(8,128)(2,1)} %bitcast.7), calls=%async_computation.2 | async-start | bytes 2359296 | tf_op jit(solution)/shard_map/all_to_all | solution.py:78
  159.0 27.6 %all-to-all-done.2 = bf16[16,48,768]{2,1,0:T(8,128)(2,1)S(1)} async-done(((bf16[16,48,768]{2,1,0:T(8,128)(2,1)}), bf16[16,48,768]{2,1,0:T(8,128)(2,1)S(1)}, u32[]{:S(2)}, u32[]{:S(2)}) %all-to-all-start.2) | async-done | bytes 1179680 | tf_op jit(solution)/shard_map/all_to_all | solution.py:78
  186.6 1.0 convolution_convert_fusion.3
  187.6 95.6 %all-reduce.2.cloned.1.call-done = bf16[2304,1536]{0,1:T(8,128)(2,1)} async-done(((bf16[2304,1536]{0,1:T(8,128)(2,1)}), bf16[2304,1536]{0,1:T(8,128)(2,1)}) %all-reduce.2.cloned.1.call-update) | async-done | bytes 7077904 | tf_op jit(solution)/shard_map/psum | solution.py:98
  283.2 1.6 dynamic-slice_convert_fusion
  284.8 1.0 copy.33
  285.8 1.0 copy.34
  (26 shorter events, 3.5 us)
Async XLA Ops:
  7.2 4.5 %copy-start = (bf16[128,768]{1,0:T(8,128)(2,1)S(1)}, bf16[128,768]{1,0:T(8,128)(2,1)}, u32[]{:S(2)}) copy-start(bf16[128,768]{1,0:T(8,128)(2,1)} %param.6) | copy-start | bytes 589828
  7.2 14.6 %copy-start.2 = (f32[128,2]{0,1:T(2,128)S(1)}, f32[128,2]{0,1:T(2,128)}, u32[]{:S(2)}) copy-start(f32[128,2]{0,1:T(2,128)} %param.9) | copy-start | bytes 3076
  7.2 14.8 %copy-start.1 = (bf16[128,768]{1,0:T(8,128)(2,1)S(1)}, bf16[128,768]{1,0:T(8,128)(2,1)}, u32[]{:S(2)}) copy-start(bf16[128,768]{1,0:T(8,128)(2,1)} %param.7) | copy-start | bytes 589828
  7.2 60.2 %all-gather.7.cloned.1.call-start = ((), (), s32[]{:S(2)}) async-start(), calls=%async_computation.5 | async-start | bytes 3760128 | tf_op jit(solution)/shard_map/all_gather | solution.py:66
  7.9 115.2 %all-gather.5.cloned.1.call-start = ((), (), s32[]{:S(2)}) async-start(), calls=%async_computation.4 | async-start | bytes 3760128 | tf_op jit(solution)/shard_map/all_gather | solution.py:67
  13.2 36.1 %all-to-all-start.1 = ((bf16[16,48,768]{2,1,0:T(8,128)(2,1)}), bf16[16,48,768]{2,1,0:T(8,128)(2,1)S(1)}, u32[]{:S(2)}, u32[]{:S(2)}) async-start(bf16[16,48,768]{2,1,0:T(8,128)(2,1)} %bitcast.4), calls=%async_computation.1 | async-start | bytes 2359296 | tf_op jit(solution)/shard_map/all_to_all | solution.py:49
  49.4 34.3 %all-to-all-start = ((bf16[16,48,768]{2,1,0:T(8,128)(2,1)}), bf16[16,48,768]{2,1,0:T(8,128)(2,1)S(1)}, u32[]{:S(2)}, u32[]{:S(2)}) async-start(bf16[16,48,768]{2,1,0:T(8,128)(2,1)} %bitcast.1), calls=%async_computation | async-start | bytes 2359296 | tf_op jit(solution)/shard_map/all_to_all | solution.py:56
  56.1 227.1 %all-reduce.2.cloned.1.call-start = ((), (), s32[]{:S(2)}) async-start(), calls=%async_computation.3 | async-start | bytes 14155776 | tf_op jit(solution)/shard_map/psum | solution.py:98
  131.6 1.8 copy-start.3
  151.5 35.1 %all-to-all-start.2 = ((bf16[16,48,768]{2,1,0:T(8,128)(2,1)}), bf16[16,48,768]{2,1,0:T(8,128)(2,1)S(1)}, u32[]{:S(2)}, u32[]{:S(2)}) async-start(bf16[16,48,768]{2,1,0:T(8,128)(2,1)} %bitcast.7), calls=%async_computation.2 | async-start | bytes 2359296 | tf_op jit(solution)/shard_map/all_to_all | solution.py:78
Sparse Core Ops, SparseCore 0:
  10.5 56.8 all-gather.6
  69.8 53.3 all-gather.4
  144.6 138.5 all-reduce.1
where the time goes:
time: 295 us; the launch traced here: 293 us
  waiting for transfers between devices  202 us (68%)
  matrix products  39.4 us (13%)
  starting transfers between devices  23.1 us (8%)
  between operations  13.8 us (5%)
  other arithmetic  9.72 us (3%)
  local copies, waits for them, and re-layouts  5.32 us (2%)
    psum x1, waiting for transfers between devices, shards(): lax.psum(jnp.concatenate([term_in, term_out], axis=1).astype(jnp.bfloat16...  95.6 us
    all_gather x1, waiting for transfers between devices, shards(): piece_out = lax.all_gather(w_out[0], 'dp', axis=0, tiled=True)  31.2 us
    all_to_all x1, waiting for transfers between devices, shards(): lax.all_to_all(slot_sum.astype(jnp.bfloat16).reshape(experts, capacity, m...  27.6 us
    all_to_all x1, waiting for transfers between devices, shards(): lax.all_to_all(rows_sent.reshape(experts, capacity, model_width), 'expert...  25.9 us
    all_gather x1, waiting for transfers between devices, shards(): piece_in = lax.all_gather(w_in[0], 'dp', axis=0, tiled=True)  11.1 us
    all_to_all x1, waiting for transfers between devices, shards(): lax.all_to_all(grads_sent.reshape(experts, capacity, model_width), 'exper...  9.28 us
    all_to_all x1, starting transfers between devices, shards(): lax.all_to_all(rows_sent.reshape(experts, capacity, model_width), 'expert...  8.59 us
    dot_general x1, matrix products, shards(): lax.dot_general(grads_in, piece_out, (((1,), (1,)), ((), ())), preferred_...  8.43 us
  transfers between devices with their start and end apart: 6, of which 6 were waited for; matrix products, arithmetic and copies ran while one was open for 10% of the time, Pallas kernels for 0%

commit v1 on v0

--- a/solution.py
+++ b/solution.py
@@ -45,24 +45,13 @@
     rows_sent = jnp.dot(route_mat, tokens, preferred_element_type=jnp.float32).astype(jnp.bfloat16)
     grad_rows = jnp.dot(route_mat, cotangent, preferred_element_type=jnp.float32)
     grads_sent = (gate_slot[:, None] * grad_rows).astype(jnp.bfloat16)
-    rows_recv, grads_recv = (
-        lax.all_to_all(
-            rows_sent.reshape(experts, capacity, model_width),
-            "expert",
-            split_axis=0,
-            concat_axis=0,
-            tiled=True,
-        ),
-        lax.all_to_all(
-            grads_sent.reshape(experts, capacity, model_width),
-            "expert",
-            split_axis=0,
-            concat_axis=0,
-            tiled=True,
-        ),
+    both_sent = jnp.stack(
+        [rows_sent.reshape(experts, capacity, model_width), grads_sent.reshape(experts, capacity, model_width)],
+        axis=1,
     )
-    rows_in = rows_recv.reshape(slot_rows, model_width)
-    grads_in = grads_recv.reshape(slot_rows, model_width)
+    both_recv = lax.all_to_all(both_sent, "expert", split_axis=0, concat_axis=0, tiled=True)
+    rows_in = both_recv[:, 0].reshape(slot_rows, model_width)
+    grads_in = both_recv[:, 1].reshape(slot_rows, model_width)
     piece_in = lax.all_gather(w_in[0], "dp", axis=0, tiled=True)
     piece_out = lax.all_gather(w_out[0], "dp", axis=0, tiled=True)
     pre = lax.dot_general(
@@ -95,12 +84,10 @@
     term_out = lax.dot_general(
         acts_all, grads_in, (((0,), (0,)), ((), ())), preferred_element_type=jnp.float32
     )
-    summed = lax.psum(
-        jnp.concatenate([term_in, term_out], axis=1).astype(jnp.bfloat16), "dp"
-    ).astype(jnp.float32)
-    own_rows = lax.dynamic_slice_in_dim(summed, lax.axis_index("dp") * shard_rows, shard_rows, 0)
-    grad_in = own_rows[:, :model_width][None]
-    grad_out = own_rows[:, model_width:][None]
+    grad_in = lax.psum_scatter(term_in.astype(jnp.bfloat16), "dp", scatter_dimension=0, tiled=True)
+    grad_out = lax.psum_scatter(term_out.astype(jnp.bfloat16), "dp", scatter_dimension=0, tiled=True)
+    grad_in = grad_in.astype(jnp.float32)[None]
+    grad_out = grad_out.astype(jnp.float32)[None]
     return (d_tokens, grad_in, grad_out)
 
 

time: 295 us -> 300 us (1.017)
  blocking collectives: 0 us -> 100 us
  waiting for transfers between devices: 202 us -> 142 us
  starting transfers between devices: 23.1 us -> 0.16 us
  matrix products: 39.4 us -> 32 us
  other arithmetic: 9.72 us -> 6.06 us
    reduce_scatter x0 -> x2, waiting for transfers between devices: none -> 108 us  [the longest x1 82.8 us: shards(): lax.psum_scatter(term_in.astype(jnp.bfloat16), 'dp', scatter_dimension=0,...]
    all_to_all x0 -> x2, blocking collectives: none -> 100 us  [the longest x1 63 us: shards(): lax.all_to_all(both_sent, 'expert', split_axis=0, concat_axis=0, tiled=True)]
    psum x1 -> x0, waiting for transfers between devices: 95.6 us -> none  [shards(): lax.psum(jnp.concatenate([term_in, term_out], axis=1).astype(jnp.bfloat16...]
    all_to_all x3 -> x0, waiting for transfers between devices: 62.7 us -> none  [the longest x1 27.6 us: shards(): lax.all_to_all(slot_sum.astype(jnp.bfloat16).reshape(experts, capacity, m...]
    all_to_all x3 -> x0, starting transfers between devices: 22.8 us -> none  [the longest x1 8.59 us: shards(): lax.all_to_all(rows_sent.reshape(experts, capacity, model_width), 'expert...]
    all_gather x1, waiting for transfers between devices: 11.1 us -> 0.02 us  [shards(): piece_in = lax.all_gather(w_in[0], 'dp', axis=0, tiled=True)]
    concatenate x1 -> x0, other arithmetic: 6.45 us -> none  [shards(): jnp.concatenate([term_in, term_out], axis=1).astype(jnp.bfloat16)]
    broadcast_in_dim x0 -> x2, other arithmetic: none -> 3.45 us  [the longest x1 1.73 us: shards(): grad_out = grad_out.astype(jnp.float32)[None]]
  transfers between devices with their start and end apart: 6 -> 4, of which waited for: 6 -> 3; matrix products, arithmetic and copies ran while one was open for 10% -> 13% of each run, Pallas kernels for 0% -> 0%
where the time goes in v1:
time: 300 us
  waiting for transfers between devices  142 us (47%)
  blocking collectives  100 us (33%)
  matrix products  32 us (11%)
  between operations  13.9 us (5%)
  local copies, waits for them, and re-layouts  6.33 us (2%)
  other arithmetic  6.06 us (2%)
    reduce_scatter x1, waiting for transfers between devices, shards(): lax.psum_scatter(term_in.astype(jnp.bfloat16), 'dp', scatter_dimension=0,...  82.8 us
    all_to_all x1, blocking collectives, shards(): lax.all_to_all(both_sent, 'expert', split_axis=0, concat_axis=0, tiled=True)  63 us
    all_to_all x1, blocking collectives, shards(): lax.all_to_all(slot_sum.astype(jnp.bfloat16).reshape(experts, capacity, m...  37.1 us
    all_gather x1, waiting for transfers between devices, shards(): piece_out = lax.all_gather(w_out[0], 'dp', axis=0, tiled=True)  31.9 us
    reduce_scatter x1, waiting for transfers between devices, shards(): lax.psum_scatter(term_out.astype(jnp.bfloat16), 'dp', scatter_dimension=0...  25.5 us
    dot_general x1, matrix products, shards(): lax.dot_general(grads_in, piece_out, (((1,), (1,)), ((), ())), preferred_...  8.36 us
  transfers between devices with their start and end apart: 4, of which 3 were waited for; matrix products, arithmetic and copies ran while one was open for 13% of the time, Pallas kernels for 0%

profile of v1, /device:TPU:32, one launch (start us, length us, event | category | flops | bytes accessed | tf_op | source)
XLA Modules:
  0.0 300.2 jit_solution(16252325126916230375)
XLA Ops:
  7.2 0.7 all-gather.7.cloned.1.call-update
  8.0 0.7 all-gather.5.cloned.1.call-update
  8.7 0.8 copy.33
  9.8 0.6 reduce-window.6
  10.9 0.7 multiply_add_fusion.1
  11.7 0.9 select_reduce_fusion
  12.6 0.5 multiply_convert_fusion.2
  13.1 1.4 convolution_convert_fusion.2
  14.4 0.2 pad_maximum_fusion
  14.7 63.0 %all_to_all.10 = bf16[16,2,48,768]{3,2,1,0:T(8,128)(2,1)S(1)} all-to-all(bf16[16,2,48,768]{3,2,1,0:T(8,128)(2,1)S(1)} %pad_maximum_fusion), channel_id=1, replica_groups=mesh['dp'=16,'expert'=16] {'expert'}, dimensions={0} | all-to-all | bytes 4718592 | tf_op jit(solution)/shard_map/all_to_all | solution.py:52
  77.9 5.0 %fusion.9 = f32[768,2304]{1,0:T(8,128)S(1)} fusion(bf16[768,768]{1,0:T(8,128)(2,1)S(1)} %bitcast.58, bf16[1,2304,768]{2,1,0:T(8,128)(2,1)} %all-gather.7.cloned.1.call-done), kind=kOutput, calls=%fused_computation.14 | convolution fusion | flops 2717908992 | bytes 11796480 | tf_op jit(solution)/shard_map/dot_general | solution.py:57
  82.9 2.9 copy-done.1
  85.8 5.4 %convolution_convert_fusion = bf16[2304,768]{1,0:T(8,128)(2,1)} fusion(bf16[768,768]{1,0:T(8,128)(2,1)S(1)} %bitcast.60, f32[768,2304]{1,0:T(8,128)S(1)} %fusion.9), kind=kOutput, calls=%fused_computation.10 | convolution fusion | flops 2735603712 | bytes 11796480 | tf_op jit(solution)/shard_map/dot_general | solution.py:84
  91.2 31.9 %all-gather.5.cloned.1.call-done = bf16[1,2304,768]{2,1,0:T(8,128)(2,1)} async-done(((bf16[1,144,768]{2,1,0:T(8,128)(2,1)}), bf16[1,2304,768]{2,1,0:T(8,128)(2,1)}) %all-gather.5.cloned.1.call-update) | async-done | bytes 3538960 | tf_op jit(solution)/shard_map/all_gather | solution.py:56
  123.1 8.4 %fusion.6 = bf16[768,2304]{1,0:T(8,128)(2,1)S(1)} fusion(f32[768,2304]{1,0:T(8,128)} %copy-done.1, bf16[768,768]{1,0:T(8,128)(2,1)S(1)} %bitcast.61, bf16[1,2304,768]{2,1,0:T(8,128)(2,1)} %all-gather.5.cloned.1.call-done), kind=kOutput, calls=%fused_computation.8 | convolution fusion | flops 2751528960 | bytes 15335424 | tf_op jit(solution)/shard_map/dot_general | solution.py:61
  131.5 1.8 copy-done.2
  133.3 4.4 %convolution_convert_fusion.1 = bf16[2304,768]{1,0:T(8,128)(2,1)} fusion(bf16[768,2304]{1,0:T(8,128)(2,1)S(1)} %fusion.6, bf16[768,768]{1,0:T(8,128)(2,1)S(1)} %bitcast.59), kind=kOutput, calls=%fused_computation.11 | convolution fusion | flops 2719678464 | bytes 8257536 | tf_op jit(solution)/shard_map/dot_general | solution.py:81
  137.8 6.0 %fusion.16 = bf16[768,768]{1,0:T(8,128)(2,1)S(1)} fusion(bf16[768,2304]{1,0:T(8,128)(2,1)} %copy-done.2, bf16[1,2304,768]{2,1,0:T(8,128)(2,1)} %all-gather.7.cloned.1.call-done), kind=kOutput, calls=%fused_computation.23 | convolution fusion | flops 2718498816 | bytes 8257536 | tf_op jit(solution)/shard_map/dot_general | solution.py:65
  143.8 37.1 %all_to_all.11 = bf16[16,48,768]{2,1,0:T(8,128)(2,1)S(1)} all-to-all(bf16[16,48,768]{2,1,0:T(8,128)(2,1)S(1)} %bitcast.57), channel_id=1, replica_groups=mesh['dp'=16,'expert'=16] {'expert'}, dimensions={0} | all-to-all | bytes 2359296 | tf_op jit(solution)/shard_map/all_to_all | solution.py:67
  180.9 1.0 convolution_convert_fusion.3
  181.9 25.5 %reduce-scatter.5.cloned.1.call-done = bf16[144,768]{1,0:T(8,128)(2,1)} async-done(((bf16[2304,768]{1,0:T(8,128)(2,1)}), bf16[144,768]{1,0:T(8,128)(2,1)}) %reduce-scatter.5.cloned.1.call-update) | async-done | bytes 221200 | tf_op jit(solution)/shard_map/reduce_scatter | solution.py:88
  207.4 1.7 bitcast_convert_fusion
  209.1 82.8 %reduce-scatter.3.cloned.1.call-done = bf16[144,768]{1,0:T(8,128)(2,1)} async-done(((bf16[2304,768]{1,0:T(8,128)(2,1)}), bf16[144,768]{1,0:T(8,128)(2,1)}) %reduce-scatter.3.cloned.1.call-update) | async-done | bytes 221200 | tf_op jit(solution)/shard_map/reduce_scatter | solution.py:87
  291.9 1.7 bitcast_convert_fusion.1
  (22 shorter events, 1.3 us)
Async XLA Ops:
  7.2 5.4 %copy-start = (bf16[128,768]{1,0:T(8,128)(2,1)S(1)}, bf16[128,768]{1,0:T(8,128)(2,1)}, u32[]{:S(2)}) copy-start(bf16[128,768]{1,0:T(8,128)(2,1)} %param.7) | copy-start | bytes 589828
  7.2 70.7 %all-gather.7.cloned.1.call-start = ((), (), s32[]{:S(2)}) async-start(), calls=%async_computation.7 | async-start | bytes 3760128 | tf_op jit(solution)/shard_map/all_gather | solution.py:55
  7.9 115.2 %all-gather.5.cloned.1.call-start = ((), (), s32[]{:S(2)}) async-start(), calls=%async_computation.6 | async-start | bytes 3760128 | tf_op jit(solution)/shard_map/all_gather | solution.py:56
  8.7 198.7 %reduce-scatter.5.cloned.1.call-start = ((), (), s32[]{:S(2)}) async-start(), calls=%async_computation.5 | async-start | bytes 3760128 | tf_op jit(solution)/shard_map/reduce_scatter | solution.py:88
  82.9 2.9 copy-start.1
  91.2 200.7 %reduce-scatter.3.cloned.1.call-start = ((), (), s32[]{:S(2)}) async-start(), calls=%async_computation.4 | async-start | bytes 3760128 | tf_op jit(solution)/shard_map/reduce_scatter | solution.py:87
  131.5 1.8 copy-start.2
Sparse Core Ops, SparseCore 0:
  10.4 56.8 all-gather.6
  69.8 53.3 all-gather.4
  126.8 80.5 reduce-scatter.4
  210.9 80.9 reduce-scatter.2

commit v2 on v1

--- a/solution.py
+++ b/solution.py
@@ -84,10 +84,17 @@
     term_out = lax.dot_general(
         acts_all, grads_in, (((0,), (0,)), ((), ())), preferred_element_type=jnp.float32
     )
+    n_dp = lax.axis_size("dp")
     grad_in = lax.psum_scatter(term_in.astype(jnp.bfloat16), "dp", scatter_dimension=0, tiled=True)
-    grad_out = lax.psum_scatter(term_out.astype(jnp.bfloat16), "dp", scatter_dimension=0, tiled=True)
     grad_in = grad_in.astype(jnp.float32)[None]
-    grad_out = grad_out.astype(jnp.float32)[None]
+    parts_out = lax.all_to_all(
+        term_out.astype(jnp.bfloat16).reshape(n_dp, shard_rows, model_width),
+        "dp",
+        split_axis=0,
+        concat_axis=0,
+        tiled=True,
+    )
+    grad_out = jnp.sum(parts_out.astype(jnp.float32), axis=0)[None]
     return (d_tokens, grad_in, grad_out)
 
 

time: 300 us -> 261 us (0.87)
  blocking collectives: 100 us -> 63 us
  waiting for transfers between devices: 142 us -> 120 us
  starting transfers between devices: 0.16 us -> 12.3 us
  matrix products: 32 us -> 38.8 us
    reduce_scatter x1, waiting for transfers between devices: 82.8 us -> 6.13 us  [shards(): lax.psum_scatter(term_in.astype(jnp.bfloat16), 'dp', scatter_dimension=0,...]
    all_to_all x0 -> x2, waiting for transfers between devices: none -> 74.2 us  [the longest x1 55.6 us: shards(): lax.all_to_all(term_out.astype(jnp.bfloat16).reshape(n_dp, shard_rows, mo...]
    all_to_all x1 -> x0, blocking collectives: 37.1 us -> none  [shards(): lax.all_to_all(slot_sum.astype(jnp.bfloat16).reshape(experts, capacity, m...]
    reduce_scatter x1 -> x0, waiting for transfers between devices: 25.5 us -> none  [shards(): lax.psum_scatter(term_out.astype(jnp.bfloat16), 'dp', scatter_dimension=0...]
    all_to_all x0 -> x2, starting transfers between devices: none -> 12.2 us  [the longest x1 7.52 us: shards(): lax.all_to_all(slot_sum.astype(jnp.bfloat16).reshape(experts, capacity, m...]
    all_gather x1, waiting for transfers between devices: 31.9 us -> 38.2 us  [shards(): piece_out = lax.all_gather(w_out[0], 'dp', axis=0, tiled=True)]
    dot_general x1, matrix products: 5.4 us -> 9.04 us  [shards(): lax.dot_general(acts_all, grads_in, (((0,), (0,)), ((), ())), preferred_e...]
    reduce_sum x0 -> x1, other arithmetic: none -> 3.35 us  [shards(): grad_out = jnp.sum(parts_out.astype(jnp.float32), axis=0)[None]]
  transfers between devices with their start and end apart: 4 -> 5, of which waited for: 3 -> 4; matrix products, arithmetic and copies ran while one was open for 13% -> 13% of each run, Pallas kernels for 0% -> 0%
where the time goes in v2:
time: 261 us; the launch traced here: 259 us
  waiting for transfers between devices  120 us (46%)
  blocking collectives  63 us (24%)
  matrix products  38.8 us (15%)
  between operations  13.9 us (5%)
  starting transfers between devices  12.3 us (5%)
  other arithmetic  7.69 us (3%)
  local copies, waits for them, and re-layouts  3.35 us (1%)
    all_to_all x1, blocking collectives, shards(): lax.all_to_all(both_sent, 'expert', split_axis=0, concat_axis=0, tiled=True)  63 us
    all_to_all x1, waiting for transfers between devices, shards(): lax.all_to_all(term_out.astype(jnp.bfloat16).reshape(n_dp, shard_rows, mo...  55.6 us
    all_gather x1, waiting for transfers between devices, shards(): piece_out = lax.all_gather(w_out[0], 'dp', axis=0, tiled=True)  38.2 us
    all_to_all x1, waiting for transfers between devices, shards(): lax.all_to_all(slot_sum.astype(jnp.bfloat16).reshape(experts, capacity, m...  18.5 us
    dot_general x1, matrix products, shards(): lax.dot_general(acts_all, grads_in, (((0,), (0,)), ((), ())), preferred_e...  9.04 us
    dot_general x1, matrix products, shards(): lax.dot_general(grads_in, piece_out, (((1,), (1,)), ((), ())), preferred_...  8.33 us
    all_to_all x1, starting transfers between devices, shards(): lax.all_to_all(slot_sum.astype(jnp.bfloat16).reshape(experts, capacity, m...  7.52 us
    dot_general x1, matrix products, shards(): slot_sum = jnp.dot(dpre, piece_in, preferred_element_type=jnp.float32)  7.06 us
  transfers between devices with their start and end apart: 5, of which 4 were waited for; matrix products, arithmetic and copies ran while one was open for 13% of the time, Pallas kernels for 0%

profile of v2, /device:TPU:32, one launch (start us, length us, event | category | flops | bytes accessed | tf_op | source)
XLA Modules:
  0.0 258.9 jit_solution(9671379621295506896)
XLA Ops:
  7.2 0.7 all-gather.7.cloned.1.call-update
  8.0 0.7 all-gather.5.cloned.1.call-update
  8.7 0.8 copy.33
  9.8 0.6 reduce-window.6
  10.9 0.7 multiply_add_fusion.1
  11.7 0.9 select_reduce_fusion
  12.6 0.5 convolution_convert_fusion.2
  13.1 1.4 multiply_convert_fusion.2
  14.7 63.0 %all_to_all.15 = bf16[16,2,48,768]{3,2,1,0:T(8,128)(2,1)S(1)} all-to-all(bf16[16,2,48,768]{3,2,1,0:T(8,128)(2,1)S(1)} %pad_maximum_fusion), channel_id=1, replica_groups=mesh['dp'=16,'expert'=16] {'expert'}, dimensions={0} | all-to-all | bytes 4718592 | tf_op jit(solution)/shard_map/all_to_all | solution.py:52
  77.9 7.0 %fusion.9 = f32[768,2304]{1,0:T(8,128)} fusion(bf16[768,768]{1,0:T(8,128)(2,1)S(1)} %bitcast.59, bf16[1,2304,768]{2,1,0:T(8,128)(2,1)} %all-gather.7.cloned.1.call-done), kind=kOutput, calls=%fused_computation.15 | convolution fusion | flops 2717908992 | bytes 11796480 | tf_op jit(solution)/shard_map/dot_general | solution.py:57
  84.9 38.2 %all-gather.5.cloned.1.call-done = bf16[1,2304,768]{2,1,0:T(8,128)(2,1)} async-done(((bf16[1,144,768]{2,1,0:T(8,128)(2,1)}), bf16[1,2304,768]{2,1,0:T(8,128)(2,1)}) %all-gather.5.cloned.1.call-update) | async-done | bytes 3538960 | tf_op jit(solution)/shard_map/all_gather | solution.py:56
  123.1 8.3 %fusion.6 = bf16[768,2304]{1,0:T(8,128)(2,1)S(1)} fusion(f32[768,2304]{1,0:T(8,128)} %fusion.9, bf16[768,768]{1,0:T(8,128)(2,1)S(1)} %bitcast.57, bf16[1,2304,768]{2,1,0:T(8,128)(2,1)} %all-gather.5.cloned.1.call-done), kind=kOutput, calls=%fused_computation.8 | convolution fusion | flops 2751528960 | bytes 15335424 | tf_op jit(solution)/shard_map/dot_general | solution.py:61
  131.5 1.7 copy-done.1
  133.2 4.5 %convolution_convert_fusion.1 = bf16[2304,768]{1,0:T(8,128)(2,1)} fusion(bf16[768,2304]{1,0:T(8,128)(2,1)S(1)} %fusion.6, bf16[768,768]{1,0:T(8,128)(2,1)S(1)} %bitcast.60), kind=kOutput, calls=%fused_computation.12 | convolution fusion | flops 2719678464 | bytes 8257536 | tf_op jit(solution)/shard_map/dot_general | solution.py:81
  137.7 7.1 %fusion.16 = bf16[768,768]{1,0:T(8,128)(2,1)} fusion(bf16[768,2304]{1,0:T(8,128)(2,1)} %copy-done.1, bf16[1,2304,768]{2,1,0:T(8,128)(2,1)} %all-gather.7.cloned.1.call-done), kind=kOutput, calls=%fused_computation.24 | convolution fusion | flops 2718498816 | bytes 8257536 | tf_op jit(solution)/shard_map/dot_general | solution.py:65
  144.8 7.5 %all-to-all-start.1 = ((bf16[16,48,768]{2,1,0:T(8,128)(2,1)}), bf16[16,48,768]{2,1,0:T(8,128)(2,1)S(1)}, u32[]{:S(2)}, u32[]{:S(2)}) async-start(bf16[16,48,768]{2,1,0:T(8,128)(2,1)} %bitcast.9), calls=%async_computation.1 | async-start | bytes 2359296 | tf_op jit(solution)/shard_map/all_to_all | solution.py:67
  152.3 9.0 %convolution_convert_fusion = bf16[2304,768]{1,0:T(8,128)(2,1)} fusion(bf16[768,768]{1,0:T(8,128)(2,1)S(1)} %bitcast.58, f32[768,2304]{1,0:T(8,128)} %fusion.9), kind=kOutput, calls=%fused_computation.11 | convolution fusion | flops 2735603712 | bytes 11796480 | tf_op jit(solution)/shard_map/dot_general | solution.py:84
  161.3 18.5 %all-to-all-done.1 = bf16[16,48,768]{2,1,0:T(8,128)(2,1)S(1)} async-done(((bf16[16,48,768]{2,1,0:T(8,128)(2,1)}), bf16[16,48,768]{2,1,0:T(8,128)(2,1)S(1)}, u32[]{:S(2)}, u32[]{:S(2)}) %all-to-all-start.1) | async-done | bytes 1179680 | tf_op jit(solution)/shard_map/all_to_all | solution.py:67
  179.9 4.7 %all-to-all-start.2 = ((bf16[16,144,768]{2,1,0:T(8,128)(2,1)}), bf16[16,144,768]{2,1,0:T(8,128)(2,1)}, u32[]{:S(2)}, u32[]{:S(2)}) async-start(bf16[16,144,768]{2,1,0:T(8,128)(2,1)} %bitcast.56), calls=%async_computation.3 | async-start | bytes 7077888 | tf_op jit(solution)/shard_map/all_to_all | solution.py:90
  184.5 1.0 convolution_convert_fusion.3
  185.6 55.6 %all-to-all-done.2 = bf16[16,144,768]{2,1,0:T(8,128)(2,1)} async-done(((bf16[16,144,768]{2,1,0:T(8,128)(2,1)}), bf16[16,144,768]{2,1,0:T(8,128)(2,1)}, u32[]{:S(2)}, u32[]{:S(2)}) %all-to-all-start.2) | async-done | bytes 3538976 | tf_op jit(solution)/shard_map/all_to_all | solution.py:90
  241.2 3.4 %convert_reduce_fusion = f32[144,768]{1,0:T(8,128)} fusion(bf16[16,144,768]{2,1,0:T(8,128)(2,1)} %all-to-all-done.2), kind=kLoop, calls=%fused_computation.9 | loop fusion | flops 3428352 | bytes 3981312 | tf_op jit(solution)/shard_map/reduce_sum | solution.py:97
  244.6 6.1 %reduce-scatter.2.cloned.1.call-done = bf16[144,768]{1,0:T(8,128)(2,1)} async-done(((bf16[2304,768]{1,0:T(8,128)(2,1)}), bf16[144,768]{1,0:T(8,128)(2,1)}) %reduce-scatter.2.cloned.1.call-update) | async-done | bytes 221200 | tf_op jit(solution)/shard_map/reduce_scatter | solution.py:88
  250.7 1.7 bitcast_convert_fusion
  (20 shorter events, 1.4 us)
Async XLA Ops:
  7.2 5.4 %copy-start = (bf16[128,768]{1,0:T(8,128)(2,1)S(1)}, bf16[128,768]{1,0:T(8,128)(2,1)}, u32[]{:S(2)}) copy-start(bf16[128,768]{1,0:T(8,128)(2,1)} %param.6) | copy-start | bytes 589828
  7.2 70.7 %all-gather.7.cloned.1.call-start = ((), (), s32[]{:S(2)}) async-start(), calls=%async_computation.6 | async-start | bytes 3760128 | tf_op jit(solution)/shard_map/all_gather | solution.py:55
  7.9 115.2 %all-gather.5.cloned.1.call-start = ((), (), s32[]{:S(2)}) async-start(), calls=%async_computation.5 | async-start | bytes 3760128 | tf_op jit(solution)/shard_map/all_gather | solution.py:56
  8.7 242.0 %reduce-scatter.2.cloned.1.call-start = ((), (), s32[]{:S(2)}) async-start(), calls=%async_computation.4 | async-start | bytes 3760128 | tf_op jit(solution)/shard_map/reduce_scatter | solution.py:88
  131.5 1.7 copy-start.1
  144.8 35.1 %all-to-all-start.1 = ((bf16[16,48,768]{2,1,0:T(8,128)(2,1)}), bf16[16,48,768]{2,1,0:T(8,128)(2,1)S(1)}, u32[]{:S(2)}, u32[]{:S(2)}) async-start(bf16[16,48,768]{2,1,0:T(8,128)(2,1)} %bitcast.9), calls=%async_computation.1 | async-start | bytes 2359296 | tf_op jit(solution)/shard_map/all_to_all | solution.py:67
  179.9 61.3 %all-to-all-start.2 = ((bf16[16,144,768]{2,1,0:T(8,128)(2,1)}), bf16[16,144,768]{2,1,0:T(8,128)(2,1)}, u32[]{:S(2)}, u32[]{:S(2)}) async-start(bf16[16,144,768]{2,1,0:T(8,128)(2,1)} %bitcast.56), calls=%async_computation.3 | async-start | bytes 7077888 | tf_op jit(solution)/shard_map/all_to_all | solution.py:90
Sparse Core Ops, SparseCore 0:
  10.4 56.8 all-gather.6
  69.8 53.3 all-gather.4
  137.8 112.7 reduce-scatter.1

commit v3 on v2

--- a/solution.py
+++ b/solution.py
@@ -34,6 +34,56 @@
     return (route_mat, gate_slot)
 
 
+def grid_perm(ny, nx, dim, sign):
+    pairs = []
+    for d in range(ny * nx):
+        cy, cx = divmod(d, nx)
+        if dim == "x":
+            pairs.append((d, cy * nx + (cx + sign) % nx))
+        else:
+            pairs.append((d, ((cy + sign) % ny) * nx + cx))
+    return pairs
+
+
+def ring_gather(piece, n, perm, sign):
+    got = [None] * n
+    got[0] = piece
+    cur = piece
+    for s in range(n - 1):
+        cur = lax.ppermute(cur, "dp", perm)
+        got[(sign * (s + 1)) % n] = cur
+    return jnp.stack(got)
+
+
+def grid_gather(piece, ny, nx, first, second):
+    sizes = {"x": nx, "y": ny}
+    g1 = ring_gather(piece, sizes[first[0]], grid_perm(ny, nx, *first), first[1])
+    g2 = ring_gather(g1, sizes[second[0]], grid_perm(ny, nx, *second), second[1])
+    if first[0] == "x":
+        g2 = jnp.swapaxes(g2, 0, 1)
+    return g2
+
+
+def natural_order(rel, ny, nx):
+    me = lax.axis_index("dp")
+    cy, cx = me // nx, me % nx
+    dy, dx = jnp.divmod(jnp.arange(ny * nx, dtype=jnp.int32), nx)
+    index = ((cx - dx) % nx) * ny + (cy - dy) % ny
+    flat = rel.reshape(nx * ny, rel.shape[2], rel.shape[3])
+    return jnp.take(flat, index, axis=0).reshape(-1, rel.shape[3])
+
+
+def gather_weights(w_in, w_out, ny, nx):
+    half = w_in.shape[0] // 2
+    in_a = grid_gather(w_in[:half], ny, nx, ("x", 1), ("y", 1))
+    in_b = grid_gather(w_in[half:], ny, nx, ("x", -1), ("y", -1))
+    out_a = grid_gather(w_out[:half], ny, nx, ("y", 1), ("x", 1))
+    out_b = grid_gather(w_out[half:], ny, nx, ("y", -1), ("x", -1))
+    full_in = natural_order(jnp.concatenate([in_a, in_b], axis=2), ny, nx)
+    full_out = natural_order(jnp.concatenate([out_a, out_b], axis=2), ny, nx)
+    return full_in, full_out
+
+
 def shards(tokens, cotangent, routes, gates, w_in, w_out):
     experts = lax.axis_size("expert")
     tok_rows, model_width = tokens.shape
@@ -52,8 +102,9 @@
     both_recv = lax.all_to_all(both_sent, "expert", split_axis=0, concat_axis=0, tiled=True)
     rows_in = both_recv[:, 0].reshape(slot_rows, model_width)
     grads_in = both_recv[:, 1].reshape(slot_rows, model_width)
-    piece_in = lax.all_gather(w_in[0], "dp", axis=0, tiled=True)
-    piece_out = lax.all_gather(w_out[0], "dp", axis=0, tiled=True)
+    n_dp = lax.axis_size("dp")
+    grid_x = 4 if n_dp % 4 == 0 else 1
+    piece_in, piece_out = gather_weights(w_in[0], w_out[0], n_dp // grid_x, grid_x)
     pre = lax.dot_general(
         rows_in, piece_in, (((1,), (1,)), ((), ())), preferred_element_type=jnp.float32
     )
@@ -84,7 +135,6 @@
     term_out = lax.dot_general(
         acts_all, grads_in, (((0,), (0,)), ((), ())), preferred_element_type=jnp.float32
     )
-    n_dp = lax.axis_size("dp")
     grad_in = lax.psum_scatter(term_in.astype(jnp.bfloat16), "dp", scatter_dimension=0, tiled=True)
     grad_in = grad_in.astype(jnp.float32)[None]
     parts_out = lax.all_to_all(

time: 261 us -> 248 us (0.950)
  blocking collectives: 63 us -> 0 us
  starting transfers between devices: 12.3 us -> 63.1 us
  waiting for transfers between devices: 120 us -> 99.2 us
  other arithmetic: 7.69 us -> 24.5 us
  local copies, waits for them, and re-layouts: 3.35 us -> 13.5 us
  matrix products: 38.8 us -> 31.4 us
    all_to_all x1 -> x0, blocking collectives: 63 us -> none  [shards(): lax.all_to_all(both_sent, 'expert', split_axis=0, concat_axis=0, tiled=True)]
    ppermute x0 -> x24, starting transfers between devices: none -> 39 us  [ring_gather(): cur = lax.ppermute(cur, 'dp', perm)]
    all_gather x2 -> x0, waiting for transfers between devices: 38.3 us -> none  [the longest x1 38.2 us: shards(): piece_out = lax.all_gather(w_out[0], 'dp', axis=0, tiled=True)]
    ppermute x0 -> x24, waiting for transfers between devices: none -> 18.5 us  [ring_gather(): cur = lax.ppermute(cur, 'dp', perm)]
    all_to_all x0 -> x1, starting transfers between devices: none -> 8.72 us  [shards(): lax.all_to_all(both_sent, 'expert', split_axis=0, concat_axis=0, tiled=True)]
    gather x0 -> x2, local copies, waits for them, and re-layouts: none -> 7.35 us  [natural_order(): return jnp.take(flat, index, axis=0).reshape(-1, rel.shape[3])]
    select_n x0 -> x1, other arithmetic: none -> 5.67 us  [natural_order(): return jnp.take(flat, index, axis=0).reshape(-1, rel.shape[3])]
    concatenate x0 -> x2, other arithmetic: none -> 5.41 us  [the longest x1 3.43 us: gather_weights(): full_out = natural_order(jnp.concatenate([out_a, out_b], axis=2), ny, nx)]
  transfers between devices with their start and end apart: 5 -> 28, of which waited for: 4 -> 15; matrix products, arithmetic and copies ran while one was open for 13% -> 17% of each run, Pallas kernels for 0% -> 0%
where the time goes in v3:
time: 248 us; the launch traced here: 246 us
  waiting for transfers between devices  99.2 us (40%)
  starting transfers between devices  63.1 us (25%)
  matrix products  31.4 us (13%)
  other arithmetic  24.5 us (10%)
  between operations  14.3 us (6%)
  local copies, waits for them, and re-layouts  13.5 us (5%)
    all_to_all x1, waiting for transfers between devices, shards(): lax.all_to_all(term_out.astype(jnp.bfloat16).reshape(n_dp, shard_rows, mo...  55.4 us
    ppermute x24, starting transfers between devices, ring_gather(): cur = lax.ppermute(cur, 'dp', perm)  39 us
    ppermute x24, waiting for transfers between devices, ring_gather(): cur = lax.ppermute(cur, 'dp', perm)  18.5 us
    all_to_all x1, waiting for transfers between devices, shards(): lax.all_to_all(slot_sum.astype(jnp.bfloat16).reshape(experts, capacity, m...  18.1 us
    dot_general x1, matrix products, shards(): lax.dot_general(acts_all, grads_in, (((0,), (0,)), ((), ())), preferred_e...  9.41 us
    all_to_all x1, starting transfers between devices, shards(): lax.all_to_all(both_sent, 'expert', split_axis=0, concat_axis=0, tiled=True)  8.72 us
    all_to_all x1, starting transfers between devices, shards(): lax.all_to_all(term_out.astype(jnp.bfloat16).reshape(n_dp, shard_rows, mo...  7.99 us
    gather x2, local copies, waits for them, and re-layouts, natural_order(): return jnp.take(flat, index, axis=0).reshape(-1, rel.shape[3])  7.35 us
  transfers between devices with their start and end apart: 28, of which 15 were waited for; matrix products, arithmetic and copies ran while one was open for 17% of the time, Pallas kernels for 0%

profile of v3, /device:TPU:32, one launch (start us, length us, event | category | flops | bytes accessed | tf_op | source)
XLA Modules:
  0.0 246.0 jit_solution(9948615115740203174)
XLA Ops:
  14.6 8.7 %all-to-all-start = ((bf16[16,2,48,768]{3,2,1,0:T(8,128)(2,1)}), bf16[16,2,48,768]{3,2,1,0:T(8,128)(2,1)}, u32[]{:S(2)}, u32[]{:S(2)}) async-start(bf16[16,2,48,768]{3,2,1,0:T(8,128)(2,1)} %pad_maximum_fusion.1), calls=%async_computation | async-start | bytes 4718592 | tf_op jit(solution)/shard_map/all_to_all | solution.py:102
  26.7 3.1 %collective-permute-done.12 = bf16[72,768]{1,0:T(8,128)(2,1)S(1)} collective-permute-done((bf16[72,768]{1,0:T(8,128)(2,1)S(1)}, bf16[72,768]{1,0:T(8,128)(2,1)S(1)}, u32[]{:S(2)}, u32[]{:S(2)}) %collective-permute-start.12) | collective-permute-done | bytes 110624 | tf_op jit(solution)/shard_map/ppermute | solution.py:53
  31.8 2.9 %collective-permute-start.19 = (bf16[72,768]{1,0:T(8,128)(2,1)S(1)}, bf16[72,768]{1,0:T(8,128)(2,1)S(1)}, u32[]{:S(2)}, u32[]{:S(2)}) collective-permute-start(bf16[72,768]{1,0:T(8,128)(2,1)S(1)} %collective-permute-done.18), channel_id=1, source_target_pairs={{0,48},{16,0},{32,16},{48,32},{64,112},{80,64},{96,80},{112,96},{1... | collective-permute-start | bytes 331784 | tf_op jit(solution)/shard_map/ppermute | solution.py:53
  35.8 3.0 %collective-permute-start.6 = (bf16[72,768]{1,0:T(8,128)(2,1)S(1)}, bf16[72,768]{1,0:T(8,128)(2,1)S(1)}, u32[]{:S(2)}, u32[]{:S(2)}) collective-permute-start(bf16[72,768]{1,0:T(8,128)(2,1)S(1)} %get-tuple-element.22), channel_id=1, source_target_pairs={{0,192},{16,208},{32,224},{48,240},{64,0},{80,16},{96,32},{112,48}... | collective-permute-start | bytes 331784 | tf_op jit(solution)/shard_map/ppermute | solution.py:53
  38.8 3.3 %collective-permute-start.20 = (bf16[72,768]{1,0:T(8,128)(2,1)S(1)}, bf16[72,768]{1,0:T(8,128)(2,1)S(1)}, u32[]{:S(2)}, u32[]{:S(2)}) collective-permute-start(bf16[72,768]{1,0:T(8,128)(2,1)S(1)} %collective-permute-done.19), channel_id=1, source_target_pairs={{0,48},{16,0},{32,16},{48,32},{64,112},{80,64},{96,80},{112,96},{1... | collective-permute-start | bytes 331784 | tf_op jit(solution)/shard_map/ppermute | solution.py:53
  45.7 3.5 %collective-permute-start.21 = (bf16[4,72,768]{2,1,0:T(8,128)(2,1)S(1)}, bf16[4,72,768]{2,1,0:T(8,128)(2,1)S(1)}, u32[]{:S(2)}, u32[]{:S(2)}) collective-permute-start(bf16[4,72,768]{2,1,0:T(8,128)(2,1)S(1)} %get-tuple-element.19), channel_id=1, source_target_pairs={{0,192},{16,208},{32,224},{48,240},{64,0},{80,16},{96,32},{112,48}... | collective-permute-start | bytes 1327112 | tf_op jit(solution)/shard_map/ppermute | solution.py:53
  49.5 3.1 %collective-permute-start.8 = (bf16[72,768]{1,0:T(8,128)(2,1)S(1)}, bf16[72,768]{1,0:T(8,128)(2,1)S(1)}, u32[]{:S(2)}, u32[]{:S(2)}) collective-permute-start(bf16[72,768]{1,0:T(8,128)(2,1)S(1)} %collective-permute-done.7), channel_id=1, source_target_pairs={{0,192},{16,208},{32,224},{48,240},{64,0},{80,16},{96,32},{112,48}... | collective-permute-start | bytes 331784 | tf_op jit(solution)/shard_map/ppermute | solution.py:53
  52.6 4.0 %collective-permute-done.2 = bf16[72,768]{1,0:T(8,128)(2,1)S(1)} collective-permute-done((bf16[72,768]{1,0:T(8,128)(2,1)S(1)}, bf16[72,768]{1,0:T(8,128)(2,1)S(1)}, u32[]{:S(2)}, u32[]{:S(2)}) %collective-permute-start.2) | collective-permute-done | bytes 110624 | tf_op jit(solution)/shard_map/ppermute | solution.py:53
  62.7 3.8 %collective-permute-start.22 = (bf16[4,72,768]{2,1,0:T(8,128)(2,1)S(1)}, bf16[4,72,768]{2,1,0:T(8,128)(2,1)S(1)}, u32[]{:S(2)}, u32[]{:S(2)}) collective-permute-start(bf16[4,72,768]{2,1,0:T(8,128)(2,1)S(1)} %collective-permute-done.21), channel_id=1, source_target_pairs={{0,192},{16,208},{32,224},{48,240},{64,0},{80,16},{96,32},{112,48}... | collective-permute-start | bytes 1327112 | tf_op jit(solution)/shard_map/ppermute | solution.py:53
  73.2 3.5 %collective-permute-start.23 = (bf16[4,72,768]{2,1,0:T(8,128)(2,1)S(1)}, bf16[4,72,768]{2,1,0:T(8,128)(2,1)}, u32[]{:S(2)}, u32[]{:S(2)}) collective-permute-start(bf16[4,72,768]{2,1,0:T(8,128)(2,1)S(1)} %collective-permute-done.22), channel_id=1, source_target_pairs={{0,192},{16,208},{32,224},{48,240},{64,0},{80,16},{96,32},{112,48}... | collective-permute-start | bytes 1327112 | tf_op jit(solution)/shard_map/ppermute | solution.py:53
  90.2 3.4 %maximum_maximum_fusion = bf16[4,4,144,768]{3,2,1,0:T(8,128)(2,1)} fusion(bf16[1,4,72,768]{3,2,1,0:T(8,128)(2,1)} %bitcast.121, bf16[1,4,72,768]{3,2,1,0:T(8,128)(2,1)} %bitcast.20, bf16[1,4,72,768]{3,2,1,0:T(8,128)(2,1)} %bitcast.19, bf16[1,4,72,768]{3,2,1,0:T(8,128)(2,1)} %get-tuple-element.14, bf16[1,4,72,768]{3,2,1,0:T(8,128)(2,1)} %bitcast.13, ...), kind=kLoop, calls=%fused_computation.15 | loop fusion | flops 28311552 | bytes 7077888 | tf_op jit(solution)/shard_map/concatenate | solution.py:83
  93.6 4.6 %gather_fusion = bf16[16,144,768]{2,1,0:T(8,128)(2,1)} fusion(bf16[16,144,768]{2,1,0:T(8,128)(2,1)} %bitcast.106, s32[1024]{0:T(1024)S(1)} %pad_clamp_fusion), kind=kCustom, calls=%fused_computation.clone | custom fusion | bytes 7077952 | tf_op jit(solution)/shard_map/jit(_take)/gather | solution.py:73
  98.2 5.7 %broadcast_select_fusion.1 = (bf16[16,144,768]{2,1,0:T(8,128)(2,1)}, bf16[16,144,768]{2,1,0:T(8,128)(2,1)}) fusion(bf16[16,144,768]{2,1,0:T(8,128)(2,1)} %gather_fusion, pred[16]{0:T(512)(128)(4,1)S(1)} %get-tuple-element.8, bf16[16,144,768]{2,1,0:T(8,128)(2,1)S(1)} %gather_fusion.1), kind=kLoop, calls=%fused_computation.22 | loop fusion | flops 3538944 | bytes 14155792 | tf_op jit(solution)/shard_map/jit(_take)/select_n | solution.py:73
  106.6 2.9 %fusion.35 = f32[768,2304]{1,0:T(8,128)S(1)} fusion(bf16[768,768]{1,0:T(8,128)(2,1)S(1)} %bitcast.118, bf16[2304,768]{1,0:T(8,128)(2,1)S(1)} %bitcast.111), kind=kOutput, calls=%fused_computation.86 | convolution fusion | flops 2717908992 | bytes 11796480 | tf_op jit(solution)/shard_map/dot_general | solution.py:108
  109.6 5.7 %fusion.6 = bf16[768,2304]{1,0:T(8,128)(2,1)S(1)} fusion(f32[768,2304]{1,0:T(8,128)S(1)} %fusion.35, bf16[768,768]{1,0:T(8,128)(2,1)S(1)} %bitcast.116, bf16[2304,768]{1,0:T(8,128)(2,1)S(1)} %bitcast.113), kind=kOutput, calls=%fused_computation.10 | convolution fusion | flops 2751528960 | bytes 15335424 | tf_op jit(solution)/shard_map/dot_general | solution.py:112
  117.2 4.5 %convolution_convert_fusion.1 = bf16[2304,768]{1,0:T(8,128)(2,1)} fusion(bf16[768,2304]{1,0:T(8,128)(2,1)S(1)} %fusion.6, bf16[768,768]{1,0:T(8,128)(2,1)S(1)} %bitcast.119), kind=kOutput, calls=%fused_computation.14 | convolution fusion | flops 2719678464 | bytes 8257536 | tf_op jit(solution)/shard_map/dot_general | solution.py:132
  121.7 5.9 %convolution_convert_fusion.2 = bf16[768,768]{1,0:T(8,128)(2,1)} fusion(bf16[768,2304]{1,0:T(8,128)(2,1)} %copy-done.12, bf16[2304,768]{1,0:T(8,128)(2,1)S(1)} %bitcast.112), kind=kOutput, calls=%fused_computation.27 | convolution fusion | flops 2718498816 | bytes 8257536 | tf_op jit(solution)/shard_map/dot_general | solution.py:116
  127.6 7.3 %all-to-all-start.1 = ((bf16[16,48,768]{2,1,0:T(8,128)(2,1)}), bf16[16,48,768]{2,1,0:T(8,128)(2,1)S(1)}, u32[]{:S(2)}, u32[]{:S(2)}) async-start(bf16[16,48,768]{2,1,0:T(8,128)(2,1)} %bitcast.115), calls=%async_computation.1 | async-start | bytes 2359296 | tf_op jit(solution)/shard_map/all_to_all | solution.py:118
  135.0 9.4 %convolution_convert_fusion = bf16[2304,768]{1,0:T(8,128)(2,1)} fusion(bf16[768,768]{1,0:T(8,128)(2,1)} %bitcast.117, f32[768,2304]{1,0:T(8,128)} %copy-done.11), kind=kOutput, calls=%fused_computation.13 | convolution fusion | flops 2735603712 | bytes 11796480 | tf_op jit(solution)/shard_map/dot_general | solution.py:135
  144.4 18.1 %all-to-all-done.1 = bf16[16,48,768]{2,1,0:T(8,128)(2,1)S(1)} async-done(((bf16[16,48,768]{2,1,0:T(8,128)(2,1)}), bf16[16,48,768]{2,1,0:T(8,128)(2,1)S(1)}, u32[]{:S(2)}, u32[]{:S(2)}) %all-to-all-start.1) | async-done | bytes 1179680 | tf_op jit(solution)/shard_map/all_to_all | solution.py:118
  162.5 8.0 %all-to-all-start.2 = ((bf16[16,144,768]{2,1,0:T(8,128)(2,1)}), bf16[16,144,768]{2,1,0:T(8,128)(2,1)}, u32[]{:S(2)}, u32[]{:S(2)}) async-start(bf16[16,144,768]{2,1,0:T(8,128)(2,1)} %bitcast.114), calls=%async_computation.3 | async-start | bytes 7077888 | tf_op jit(solution)/shard_map/all_to_all | solution.py:140
  171.6 55.4 %all-to-all-done.2 = bf16[16,144,768]{2,1,0:T(8,128)(2,1)} async-done(((bf16[16,144,768]{2,1,0:T(8,128)(2,1)}), bf16[16,144,768]{2,1,0:T(8,128)(2,1)}, u32[]{:S(2)}, u32[]{:S(2)}) %all-to-all-start.2) | async-done | bytes 3538976 | tf_op jit(solution)/shard_map/all_to_all | solution.py:140
  227.0 3.3 %convert_reduce_fusion = f32[144,768]{1,0:T(8,128)} fusion(bf16[16,144,768]{2,1,0:T(8,128)(2,1)} %all-to-all-done.2), kind=kLoop, calls=%fused_computation.11 | loop fusion | flops 3428352 | bytes 3981312 | tf_op jit(solution)/shard_map/reduce_sum | solution.py:147
  230.3 7.1 %reduce-scatter.2.cloned.1.call-done = bf16[144,768]{1,0:T(8,128)(2,1)} async-done(((bf16[2304,768]{1,0:T(8,128)(2,1)}), bf16[144,768]{1,0:T(8,128)(2,1)}) %reduce-scatter.2.cloned.1.call-update) | async-done | bytes 221200 | tf_op jit(solution)/shard_map/reduce_scatter | solution.py:138
  (100 shorter events, 51.2 us)
Async XLA Ops:
  14.6 89.3 %all-to-all-start = ((bf16[16,2,48,768]{3,2,1,0:T(8,128)(2,1)}), bf16[16,2,48,768]{3,2,1,0:T(8,128)(2,1)}, u32[]{:S(2)}, u32[]{:S(2)}) async-start(bf16[16,2,48,768]{3,2,1,0:T(8,128)(2,1)} %pad_maximum_fusion.1), calls=%async_computation | async-start | bytes 4718592 | tf_op jit(solution)/shard_map/all_to_all | solution.py:102
  23.3 214.1 %reduce-scatter.2.cloned.1.call-start = ((), (), s32[]{:S(2)}) async-start(), calls=%async_computation.4 | async-start | bytes 3760128 | tf_op jit(solution)/shard_map/reduce_scatter | solution.py:138
  25.0 6.8 %collective-permute-start.18 = (bf16[72,768]{1,0:T(8,128)(2,1)S(1)}, bf16[72,768]{1,0:T(8,128)(2,1)S(1)}, u32[]{:S(2)}, u32[]{:S(2)}) collective-permute-start(bf16[72,768]{1,0:T(8,128)(2,1)S(1)} %get-tuple-element.26), channel_id=1, source_target_pairs={{0,48},{16,0},{32,16},{48,32},{64,112},{80,64},{96,80},{112,96},{1... | collective-permute-start | bytes 331784 | tf_op jit(solution)/shard_map/ppermute | solution.py:53
  30.1 8.7 %collective-permute-start = (bf16[72,768]{1,0:T(8,128)(2,1)S(1)}, bf16[72,768]{1,0:T(8,128)(2,1)S(1)}, u32[]{:S(2)}, u32[]{:S(2)}) collective-permute-start(bf16[72,768]{1,0:T(8,128)(2,1)S(1)} %get-tuple-element.21), channel_id=1, source_target_pairs={{0,64},{16,80},{32,96},{48,112},{64,128},{80,144},{96,160},{112,17... | collective-permute-start | bytes 331784 | tf_op jit(solution)/shard_map/ppermute | solution.py:53
  31.8 7.0 %collective-permute-start.19 = (bf16[72,768]{1,0:T(8,128)(2,1)S(1)}, bf16[72,768]{1,0:T(8,128)(2,1)S(1)}, u32[]{:S(2)}, u32[]{:S(2)}) collective-permute-start(bf16[72,768]{1,0:T(8,128)(2,1)S(1)} %collective-permute-done.18), channel_id=1, source_target_pairs={{0,48},{16,0},{32,16},{48,32},{64,112},{80,64},{96,80},{112,96},{1... | collective-permute-start | bytes 331784 | tf_op jit(solution)/shard_map/ppermute | solution.py:53
  35.8 7.7 %collective-permute-start.6 = (bf16[72,768]{1,0:T(8,128)(2,1)S(1)}, bf16[72,768]{1,0:T(8,128)(2,1)S(1)}, u32[]{:S(2)}, u32[]{:S(2)}) collective-permute-start(bf16[72,768]{1,0:T(8,128)(2,1)S(1)} %get-tuple-element.22), channel_id=1, source_target_pairs={{0,192},{16,208},{32,224},{48,240},{64,0},{80,16},{96,32},{112,48}... | collective-permute-start | bytes 331784 | tf_op jit(solution)/shard_map/ppermute | solution.py:53
  38.8 6.8 %collective-permute-start.1 = (bf16[72,768]{1,0:T(8,128)(2,1)S(1)}, bf16[72,768]{1,0:T(8,128)(2,1)S(1)}, u32[]{:S(2)}, u32[]{:S(2)}) collective-permute-start(bf16[72,768]{1,0:T(8,128)(2,1)S(1)} %collective-permute-done), channel_id=1, source_target_pairs={{0,64},{16,80},{32,96},{48,112},{64,128},{80,144},{96,160},{112,17... | collective-permute-start | bytes 331784 | tf_op jit(solution)/shard_map/ppermute | solution.py:53
  38.8 6.8 %collective-permute-start.20 = (bf16[72,768]{1,0:T(8,128)(2,1)S(1)}, bf16[72,768]{1,0:T(8,128)(2,1)S(1)}, u32[]{:S(2)}, u32[]{:S(2)}) collective-permute-start(bf16[72,768]{1,0:T(8,128)(2,1)S(1)} %collective-permute-done.19), channel_id=1, source_target_pairs={{0,48},{16,0},{32,16},{48,32},{64,112},{80,64},{96,80},{112,96},{1... | collective-permute-start | bytes 331784 | tf_op jit(solution)/shard_map/ppermute | solution.py:53
  42.2 20.4 %collective-permute-start.15 = (bf16[4,72,768]{2,1,0:T(8,128)(2,1)S(1)}, bf16[4,72,768]{2,1,0:T(8,128)(2,1)S(1)}, u32[]{:S(2)}, u32[]{:S(2)}) collective-permute-start(bf16[4,72,768]{2,1,0:T(8,128)(2,1)S(1)} %get-tuple-element.17), channel_id=1, source_target_pairs={{0,64},{16,80},{32,96},{48,112},{64,128},{80,144},{96,160},{112,17... | collective-permute-start | bytes 1327112 | tf_op jit(solution)/shard_map/ppermute | solution.py:53
  45.6 11.0 %collective-permute-start.2 = (bf16[72,768]{1,0:T(8,128)(2,1)S(1)}, bf16[72,768]{1,0:T(8,128)(2,1)S(1)}, u32[]{:S(2)}, u32[]{:S(2)}) collective-permute-start(bf16[72,768]{1,0:T(8,128)(2,1)S(1)} %collective-permute-done.1), channel_id=1, source_target_pairs={{0,64},{16,80},{32,96},{48,112},{64,128},{80,144},{96,160},{112,17... | collective-permute-start | bytes 331784 | tf_op jit(solution)/shard_map/ppermute | solution.py:53
  45.7 17.0 %collective-permute-start.21 = (bf16[4,72,768]{2,1,0:T(8,128)(2,1)S(1)}, bf16[4,72,768]{2,1,0:T(8,128)(2,1)S(1)}, u32[]{:S(2)}, u32[]{:S(2)}) collective-permute-start(bf16[4,72,768]{2,1,0:T(8,128)(2,1)S(1)} %get-tuple-element.19), channel_id=1, source_target_pairs={{0,192},{16,208},{32,224},{48,240},{64,0},{80,16},{96,32},{112,48}... | collective-permute-start | bytes 1327112 | tf_op jit(solution)/shard_map/ppermute | solution.py:53
  49.5 9.8 %collective-permute-start.8 = (bf16[72,768]{1,0:T(8,128)(2,1)S(1)}, bf16[72,768]{1,0:T(8,128)(2,1)S(1)}, u32[]{:S(2)}, u32[]{:S(2)}) collective-permute-start(bf16[72,768]{1,0:T(8,128)(2,1)S(1)} %collective-permute-done.7), channel_id=1, source_target_pairs={{0,192},{16,208},{32,224},{48,240},{64,0},{80,16},{96,32},{112,48}... | collective-permute-start | bytes 331784 | tf_op jit(solution)/shard_map/ppermute | solution.py:53
  57.5 11.1 %collective-permute-start.3 = (bf16[4,72,768]{2,1,0:T(8,128)(2,1)S(1)}, bf16[4,72,768]{2,1,0:T(8,128)(2,1)S(1)}, u32[]{:S(2)}, u32[]{:S(2)}) collective-permute-start(bf16[4,72,768]{2,1,0:T(8,128)(2,1)S(1)} %get-tuple-element.13), channel_id=1, source_target_pairs={{0,16},{16,32},{32,48},{48,0},{64,80},{80,96},{96,112},{112,64},{1... | collective-permute-start | bytes 1327112 | tf_op jit(solution)/shard_map/ppermute | solution.py:53
  60.1 10.2 %collective-permute-start.9 = (bf16[4,72,768]{2,1,0:T(8,128)(2,1)S(1)}, bf16[4,72,768]{2,1,0:T(8,128)(2,1)S(1)}, u32[]{:S(2)}, u32[]{:S(2)}) collective-permute-start(bf16[4,72,768]{2,1,0:T(8,128)(2,1)S(1)} %get-tuple-element.15), channel_id=1, source_target_pairs={{0,48},{16,0},{32,16},{48,32},{64,112},{80,64},{96,80},{112,96},{1... | collective-permute-start | bytes 1327112 | tf_op jit(solution)/shard_map/ppermute | solution.py:53
  62.6 10.4 %collective-permute-start.16 = (bf16[4,72,768]{2,1,0:T(8,128)(2,1)S(1)}, bf16[4,72,768]{2,1,0:T(8,128)(2,1)S(1)}, u32[]{:S(2)}, u32[]{:S(2)}) collective-permute-start(bf16[4,72,768]{2,1,0:T(8,128)(2,1)S(1)} %collective-permute-done.15), channel_id=1, source_target_pairs={{0,64},{16,80},{32,96},{48,112},{64,128},{80,144},{96,160},{112,17... | collective-permute-start | bytes 1327112 | tf_op jit(solution)/shard_map/ppermute | solution.py:53
  62.7 10.6 %collective-permute-start.22 = (bf16[4,72,768]{2,1,0:T(8,128)(2,1)S(1)}, bf16[4,72,768]{2,1,0:T(8,128)(2,1)S(1)}, u32[]{:S(2)}, u32[]{:S(2)}) collective-permute-start(bf16[4,72,768]{2,1,0:T(8,128)(2,1)S(1)} %collective-permute-done.21), channel_id=1, source_target_pairs={{0,192},{16,208},{32,224},{48,240},{64,0},{80,16},{96,32},{112,48}... | collective-permute-start | bytes 1327112 | tf_op jit(solution)/shard_map/ppermute | solution.py:53
  68.6 10.4 %collective-permute-start.4 = (bf16[4,72,768]{2,1,0:T(8,128)(2,1)S(1)}, bf16[4,72,768]{2,1,0:T(8,128)(2,1)}, u32[]{:S(2)}, u32[]{:S(2)}) collective-permute-start(bf16[4,72,768]{2,1,0:T(8,128)(2,1)S(1)} %collective-permute-done.3), channel_id=1, source_target_pairs={{0,16},{16,32},{32,48},{48,0},{64,80},{80,96},{96,112},{112,64},{1... | collective-permute-start | bytes 1327112 | tf_op jit(solution)/shard_map/ppermute | solution.py:53
  70.3 9.5 %collective-permute-start.10 = (bf16[4,72,768]{2,1,0:T(8,128)(2,1)S(1)}, bf16[4,72,768]{2,1,0:T(8,128)(2,1)}, u32[]{:S(2)}, u32[]{:S(2)}) collective-permute-start(bf16[4,72,768]{2,1,0:T(8,128)(2,1)S(1)} %collective-permute-done.9), channel_id=1, source_target_pairs={{0,48},{16,0},{32,16},{48,32},{64,112},{80,64},{96,80},{112,96},{1... | collective-permute-start | bytes 1327112 | tf_op jit(solution)/shard_map/ppermute | solution.py:53
  73.1 9.9 %collective-permute-start.17 = (bf16[4,72,768]{2,1,0:T(8,128)(2,1)S(1)}, bf16[4,72,768]{2,1,0:T(8,128)(2,1)}, u32[]{:S(2)}, u32[]{:S(2)}) collective-permute-start(bf16[4,72,768]{2,1,0:T(8,128)(2,1)S(1)} %collective-permute-done.16), channel_id=1, source_target_pairs={{0,64},{16,80},{32,96},{48,112},{64,128},{80,144},{96,160},{112,17... | collective-permute-start | bytes 1327112 | tf_op jit(solution)/shard_map/ppermute | solution.py:53
  73.2 10.9 %collective-permute-start.23 = (bf16[4,72,768]{2,1,0:T(8,128)(2,1)S(1)}, bf16[4,72,768]{2,1,0:T(8,128)(2,1)}, u32[]{:S(2)}, u32[]{:S(2)}) collective-permute-start(bf16[4,72,768]{2,1,0:T(8,128)(2,1)S(1)} %collective-permute-done.22), channel_id=1, source_target_pairs={{0,192},{16,208},{32,224},{48,240},{64,0},{80,16},{96,32},{112,48}... | collective-permute-start | bytes 1327112 | tf_op jit(solution)/shard_map/ppermute | solution.py:53
  79.0 11.2 %collective-permute-start.5 = (bf16[4,72,768]{2,1,0:T(8,128)(2,1)}, bf16[4,72,768]{2,1,0:T(8,128)(2,1)}, u32[]{:S(2)}, u32[]{:S(2)}) collective-permute-start(bf16[4,72,768]{2,1,0:T(8,128)(2,1)} %collective-permute-done.4), channel_id=1, source_target_pairs={{0,16},{16,32},{32,48},{48,0},{64,80},{80,96},{96,112},{112,64},{1... | collective-permute-start | bytes 1327112 | tf_op jit(solution)/shard_map/ppermute | solution.py:53
  79.8 10.4 %collective-permute-start.11 = (bf16[4,72,768]{2,1,0:T(8,128)(2,1)}, bf16[4,72,768]{2,1,0:T(8,128)(2,1)}, u32[]{:S(2)}, u32[]{:S(2)}) collective-permute-start(bf16[4,72,768]{2,1,0:T(8,128)(2,1)} %collective-permute-done.10), channel_id=1, source_target_pairs={{0,48},{16,0},{32,16},{48,32},{64,112},{80,64},{96,80},{112,96},{1... | collective-permute-start | bytes 1327112 | tf_op jit(solution)/shard_map/ppermute | solution.py:53
  127.6 34.9 %all-to-all-start.1 = ((bf16[16,48,768]{2,1,0:T(8,128)(2,1)}), bf16[16,48,768]{2,1,0:T(8,128)(2,1)S(1)}, u32[]{:S(2)}, u32[]{:S(2)}) async-start(bf16[16,48,768]{2,1,0:T(8,128)(2,1)} %bitcast.115), calls=%async_computation.1 | async-start | bytes 2359296 | tf_op jit(solution)/shard_map/all_to_all | solution.py:118
  162.5 64.5 %all-to-all-start.2 = ((bf16[16,144,768]{2,1,0:T(8,128)(2,1)}), bf16[16,144,768]{2,1,0:T(8,128)(2,1)}, u32[]{:S(2)}, u32[]{:S(2)}) async-start(bf16[16,144,768]{2,1,0:T(8,128)(2,1)} %bitcast.114), calls=%async_computation.3 | async-start | bytes 7077888 | tf_op jit(solution)/shard_map/all_to_all | solution.py:140
  (17 other events, 181.5 us)
Sparse Core Ops, SparseCore 0:
  121.8 115.5 reduce-scatter.1
